TPU v7x, 128 devices: a whole 4x4x4 slice. The times are simulated.
128 devices in a mesh: req: 8 (over x, core), kv: 16 (over y, z).
Axes of the slice: x: 4, y: 4, z: 4, core: 2. Of those that a mesh axis runs over, the one named last changes fastest.
Arguments:
- x_steps: bfloat16 [4, 1024, 1536], P(None, ('req', 'kv')), may hold values from -6 to 6
- lengths: int32 [128], replicated, may hold values from 16 to 8192
- perm: int32 [128], replicated, may hold values from 0 to 127, as said below
- parents: int32 [4, 1024], replicated, may hold values from 0 to 7
- table: int32 [1024, 9], P(('req', 'kv')), may hold values from 0 to 9215, as said below
- pool: bfloat16 [9216, 128, 256], P(('req', 'kv')), may hold values from -900 to 900
- norm_attn: float32 [1536], replicated, may hold values from 0.1 to 1.9
- w_query: bfloat16 [1536, 1536], replicated, may hold values from -0.15625 to 0.15625
- w_keyval: bfloat16 [1536, 256], replicated, may hold values from -0.15625 to 0.15625
- w_out: bfloat16 [1536, 1536], replicated, may hold values from -0.15625 to 0.15625
- norm_mlp: float32 [1536], replicated, may hold values from 0.1 to 1.9
- w_gate: bfloat16 [1536, 4608], P(None, 'kv'), may hold values from -0.15625 to 0.15625
- w_up: bfloat16 [1536, 4608], P(None, 'kv'), may hold values from -0.15625 to 0.15625
- w_down: bfloat16 [4608, 1536], P('kv'), may hold values from -0.09375 to 0.09375
Outputs:
- outputs: bfloat16 [4, 1024, 1536], P(None, ('req', 'kv'))
Inputs may be any that keep to these rules, and one draw needn't show every extreme that they name: perm is a permutation with perm[s] % 16 == s % 16; among the 8 slots s with one s // 16 and one s % 16 // 8, every req index occurs as perm[s] // 16 exactly once. The entries of row b lie in [(b // 8) * 72, (b // 8 + 1) * 72); no page appears twice in the table.
All inputs are finite; a program needn't handle non-finite values.
Results may differ from a plain program's by a relative error of at most 0.02.
Values may be sent and summed in bfloat16 or wider, within the bound.
No kernel may reach another device: no remote copies, remote signals or barrier semaphores. Data moves between devices by JAX's collectives and lax.ppermute only.
A program may use at most 192 MiB of HBM per device.

v0:
```python
import jax
import jax.numpy as jnp
from jax import lax
from jax.sharding import PartitionSpec as P

WINDOW = 1024
PAGE = 128
BEAMS = 8
EPSILON = 1e-06
NEGATIVE = -1e30


def member_of(beam_index, half_index, halves):
    return beam_index % 2 + 2 * half_index + 2 * halves * (beam_index // 2)


def rms_round(values, gain):
    wide = values.astype(jnp.float32)
    mean_square = jnp.mean(wide * wide, axis=-1, keepdims=True)
    return (wide * lax.rsqrt(mean_square + EPSILON) * gain).astype(jnp.bfloat16)


def rank_within(labels, offsets):
    earlier = (labels[None, :] == labels[:, None]) & (offsets[None, :] < offsets[:, None])
    return jnp.sum(earlier.astype(jnp.int32), axis=1)


def follow(index, table):
    picks = index[:, None, :] == jnp.arange(BEAMS, dtype=jnp.int32)[None, :, None]
    return jnp.sum(jnp.where(picks, table[None, :, :], 0), axis=1)


def pick_rows(index, table):
    picks = index[:, None, :] == jnp.arange(BEAMS, dtype=jnp.int32)[None, :, None]
    return jnp.sum(jnp.where(picks[..., None], table[None, :, :, :], 0), axis=1).astype(table.dtype)


def on_device(
    x_steps,
    lengths,
    perm,
    parents,
    table,
    pool,
    norm_attn,
    w_query,
    w_keyval,
    w_out,
    norm_mlp,
    w_gate,
    w_up,
    w_down,
):
    steps, rows, width = x_steps.shape
    head_dim = pool.shape[2] // 2
    heads = w_query.shape[1] // head_dim
    qwidth = heads * head_dim
    span = table.shape[1] * pool.shape[1]
    req_count = lax.axis_size("req")
    kv_count = lax.axis_size("kv")
    group = lax.axis_index("req")
    member = lax.axis_index("kv")
    halves = kv_count // BEAMS
    half = member // 2 % halves
    beam = member % 2 + 2 * (member // (2 * halves))
    per_group = halves * rows
    group_rows = kv_count * rows
    quota = rows // req_count
    offsets = jnp.arange(rows, dtype=jnp.int32)
    slot_ids = group * per_group + half * rows + offsets
    placed = lax.dynamic_slice_in_dim(perm.reshape(req_count, per_group), half * rows, rows, 1)
    serving = lax.dynamic_index_in_dim(placed, group, 0, keepdims=False)
    target = jnp.sum(
        jnp.where(placed == slot_ids[None, :], jnp.arange(req_count, dtype=jnp.int32)[:, None], 0),
        axis=0,
    )
    anchor = serving // per_group
    send_order = jnp.argsort(target * rows + offsets)
    outgoing = x_steps[:, send_order].reshape(steps, req_count, quota, width)
    arrived = lax.all_to_all(outgoing, "req", split_axis=1, concat_axis=1, tiled=True).reshape(
        steps, rows, width
    )
    inputs = arrived[:, anchor * quota + rank_within(anchor, offsets)]
    normed = rms_round(inputs.reshape(steps * rows, width), norm_attn)
    query = jnp.dot(normed, w_query, preferred_element_type=jnp.float32).astype(jnp.bfloat16)
    fresh = jnp.dot(normed, w_keyval, preferred_element_type=jnp.float32).astype(jnp.bfloat16)
    packed = jnp.concatenate([query, fresh], axis=-1).reshape(steps, rows, qwidth + 2 * head_dim)
    gathered = lax.all_gather(packed, "kv", axis=0)
    mine = gathered.reshape((BEAMS // 2, halves, 2) + packed.shape)
    mine = lax.dynamic_index_in_dim(mine, half, 1, keepdims=False).reshape((BEAMS,) + packed.shape)
    queries = mine[..., :qwidth].reshape(BEAMS, steps, rows, heads, head_dim)
    entries = mine[..., qwidth:]
    family = lax.dynamic_slice_in_dim(parents, group * group_rows, group_rows, 1).reshape(
        (steps, BEAMS // 2, halves, 2, rows)
    )
    family = lax.dynamic_index_in_dim(family, half, 2, keepdims=False).reshape(steps, BEAMS, rows)
    own = jnp.broadcast_to(jnp.arange(BEAMS, dtype=jnp.int32)[:, None], (BEAMS, rows))
    cache_beam = own
    sources = []
    cache_beams = []
    listed = []
    for step_index in range(steps):
        cache_beam = follow(family[step_index], cache_beam)
        sources = [follow(family[step_index], source) for source in sources] + [own]
        cache_beams.append(cache_beam)
        picked = [pick_rows(source, entries[:, s]) for s, source in enumerate(sources)]
        picked += [jnp.zeros_like(picked[0])] * (steps - 1 - step_index)
        listed.append(jnp.stack(picked))
    held = jnp.stack(cache_beams, axis=1) == beam
    listed = jnp.stack(listed)
    length = lengths[serving]
    first_page = jnp.maximum(length - WINDOW + 1, 0) // PAGE
    key_pos = first_page[:, None] * PAGE + jnp.arange(span, dtype=jnp.int32)[None, :]
    device = group * kv_count + member
    pages = pool[table - device * pool.shape[0]].reshape(rows, span, 2 * head_dim)
    keys = pages[:, :, :head_dim]
    values = pages[:, :, head_dim:]
    scale = head_dim ** (-0.5)
    scores = (
        jnp.einsum("jtrhd,rkd->jtrhk", queries, keys, preferred_element_type=jnp.float32) * scale
    )
    step_ids = jnp.arange(steps, dtype=jnp.int32)
    allowed = (key_pos[None, :, :] < length[None, :, None]) & (
        key_pos[None, :, :] > length[None, :, None] + step_ids[:, None, None] - WINDOW
    )
    scores = jnp.where(allowed[None, :, :, None, :], scores, NEGATIVE)
    high_c = jnp.max(scores, axis=-1)
    weights = jnp.exp(scores - high_c[..., None]).astype(jnp.bfloat16)
    total_c = jnp.sum(weights.astype(jnp.float32), axis=-1)
    sum_c = jnp.einsum("jtrhk,rkd->jtrhd", weights, values, preferred_element_type=jnp.float32)
    new_keys = listed[..., :head_dim]
    new_values = listed[..., head_dim:]
    fresh_scores = (
        jnp.einsum("jtrhd,tsjrd->jtrhs", queries, new_keys, preferred_element_type=jnp.float32)
        * scale
    )
    counted = step_ids[None, :] <= step_ids[:, None]
    fresh_scores = jnp.where(counted[None, :, None, None, :], fresh_scores, NEGATIVE)
    high_n = jnp.max(fresh_scores, axis=-1)
    fresh_weights = jnp.exp(fresh_scores - high_n[..., None]).astype(jnp.bfloat16)
    fresh_weights = jnp.where(counted[None, :, None, None, :], fresh_weights, 0)
    total_n = jnp.sum(fresh_weights.astype(jnp.float32), axis=-1)
    sum_n = jnp.einsum(
        "jtrhs,tsjrd->jtrhd", fresh_weights, new_values, preferred_element_type=jnp.float32
    )
    highest = jnp.maximum(high_c, high_n)
    scale_c = jnp.exp(high_c - highest)
    scale_n = jnp.exp(high_n - highest)
    totals = total_c * scale_c + total_n * scale_n
    weighted = sum_c * scale_c[..., None] + sum_n * scale_n[..., None]
    attended = (
        (weighted / totals[..., None]).astype(jnp.bfloat16).reshape(BEAMS, steps, rows, qwidth)
    )
    attended = jnp.where(held[..., None], attended, jnp.zeros_like(attended))
    spread = attended.reshape(BEAMS // 2, 1, 2, steps, rows, qwidth)
    in_half = (jnp.arange(halves, dtype=jnp.int32) == half)[None, :, None, None, None, None]
    outgoing_att = jnp.where(in_half, spread, jnp.zeros_like(spread)).reshape(
        kv_count, steps, rows, qwidth
    )
    received = lax.all_to_all(outgoing_att, "kv", split_axis=0, concat_axis=0, tiled=True)
    attended_own = jnp.sum(received.astype(jnp.float32), axis=0).astype(jnp.bfloat16)
    current = inputs.reshape(steps * rows, width)
    residual = (
        current.astype(jnp.float32)
        + jnp.dot(
            attended_own.reshape(steps * rows, qwidth), w_out, preferred_element_type=jnp.float32
        )
    ).astype(jnp.bfloat16)
    mlp_in = lax.all_gather(rms_round(residual, norm_mlp), "kv", axis=0, tiled=True)
    gate = jnp.dot(mlp_in, w_gate, preferred_element_type=jnp.float32)
    upward = jnp.dot(mlp_in, w_up, preferred_element_type=jnp.float32)
    hidden = (jax.nn.gelu(gate, approximate=True) * upward).astype(jnp.bfloat16)
    terms = jnp.dot(hidden, w_down, preferred_element_type=jnp.float32).astype(jnp.bfloat16)
    terms = terms.reshape(kv_count, steps * rows, width)
    partial = lax.all_to_all(terms, "kv", split_axis=0, concat_axis=0, tiled=True)
    summed = jnp.sum(partial.astype(jnp.float32), axis=0)
    finished = (
        (residual.astype(jnp.float32) + summed).astype(jnp.bfloat16).reshape(steps, rows, width)
    )
    back_order = jnp.argsort(anchor * rows + offsets)
    leaving = finished[:, back_order].reshape(steps, req_count, quota, width)
    returned = lax.all_to_all(leaving, "req", split_axis=1, concat_axis=1, tiled=True).reshape(
        steps, rows, width
    )
    return returned[:, target * quota + rank_within(target, offsets)]


def solution(mesh):
    in_specs = (
        P(None, ("req", "kv"), None),
        P(),
        P(),
        P(),
        P(("req", "kv"), None),
        P(("req", "kv"), None, None),
        P(),
        P(),
        P(),
        P(),
        P(),
        P(None, "kv"),
        P(None, "kv"),
        P("kv", None),
    )
    out_specs = P(None, ("req", "kv"), None)
    return jax.shard_map(
        on_device, mesh=mesh, in_specs=in_specs, out_specs=out_specs, check_vma=False
    )
```

profile of v0, /device:TPU:1, one launch (start us, length us, event | category | flops | bytes accessed | tf_op | source)
XLA Modules:
  0.0 238.4 jit_solution(9731133063465071926)
XLA Ops:
  6.5 0.8 reshape.452
  7.5 1.0 sort.31
  8.5 1.7 gather_fusion
  10.3 0.7 copy.127
  10.9 5.8 %all-to-all-start = ((bf16[4,8,1,1536]{3,0,2,1:T(4,128)(2,1)}), bf16[4,8,1,1536]{3,0,2,1:T(4,128)(2,1)S(1)}, u32[]{:S(2)}, u32[]{:S(2)}) async-start(bf16[4,8,1,1536]{3,0,2,1:T(4,128)(2,1)} %copy.127), calls=%async_computation | async-start | bytes 196608 | tf_op jit(solution)/shard_map/all_to_all | solution.py:80
  16.9 0.7 compare_select_fusion
  17.9 0.7 constant_dynamic-slice_fusion.4
  18.8 1.3 gather_fusion.3
  20.2 1.6 all-to-all-done
  22.7 1.4 convolution_convert_fusion.2
  24.1 3.3 %convolution_convert_fusion.1 = bf16[32,1536]{1,0:T(8,128)(2,1)S(1)} fusion(bf16[1536,1536]{1,0:T(8,128)(2,1)} %param.21, f32[4,8,1536]{2,0,1:T(4,128)S(1)} %convert_bitcast_fusion, f32[1536]{0:T(1024)} %param.20, f32[32]{0:T(128)S(1)} %rsqrt.20), kind=kOutput, calls=%fused_computation.19 | convolution fusion | flops 151191552 | bytes 5019776 | tf_op jit(solution)/shard_map/dot_general | solution.py:85
  28.2 7.8 %gather_fusion.2 = bf16[72,128,256]{2,1,0:T(8,128)(2,1)} fusion(bf16[72,128,256]{2,1,0:T(8,128)(2,1)} %param.19, s32[1024]{0:T(1024)S(1)} %pad_clamp_fusion.3), kind=kCustom, calls=%fused_computation.2 | custom fusion | bytes 9437472 | tf_op jit(solution)/shard_map/gather | solution.py:115
  36.7 35.6 %all-gather.3.cloned.1.call-done = bf16[16,4,8,1792]{3,2,1,0:T(8,128)(2,1)} async-done(((bf16[1,4,8,1792]{3,2,1,0:T(8,128)(2,1)}), bf16[16,4,8,1792]{3,2,1,0:T(8,128)(2,1)}) %all-gather.3.cloned.1.call-update) | async-done | bytes 1835024 | tf_op jit(solution)/shard_map/all_gather | solution.py:88
  72.3 1.4 constant_dynamic-slice_fusion.1
  73.8 0.8 select_reduce_fusion.9
  77.9 1.9 fusion.25
  79.8 8.5 %fusion = (f32[8,4,8,12]{3,1,0,2:T(4,128)S(1)}, f32[8,1152,8,4,12]{1,4,3,2,0:T(8,128)}) fusion(pred[4,8,1152]{2,0,1:T(4,128)(4,1)S(1)} %compare_and_fusion, bf16[8,4,8,12,128]{4,2,3,1,0:T(8,128)(2,1)S(1)} %slice_bitcast_fusion.6, bf16[8,1152,256]{2,1,0:T(8,128)(2,1)S(1)} %bitcast.164), kind=kOutput, calls=%fused_computation.10 | convolution fusion | flops 916583424 | bytes 17350656 | tf_op jit(solution)/shard_map/jtrhd,rkd->jtrhk/dot_general | solution.py:120
  88.3 11.0 %convert_reduce_fusion = f32[8,4,8,12]{3,1,0,2:T(4,128)S(1)} fusion(f32[8,4,8,12]{3,1,0,2:T(4,128)S(1)} %get-tuple-element.56, f32[8,1152,8,4,12]{1,4,3,2,0:T(8,128)} %get-tuple-element.57, pred[4,8,1152]{2,0,1:T(4,128)(4,1)S(1)} %compare_and_fusion), kind=kLoop, calls=%fused_computation.8 | loop fusion | flops 17691648 | bytes 14217216 | tf_op jit(solution)/shard_map/reduce_sum | solution.py:129
  99.6 9.7 %fusion.6 = bf16[8,4,8,12,128]{4,3,1,0,2:T(8,128)(2,1)S(1)} fusion(f32[8,4,8,12,128]{4,3,1,0,2:T(8,128)} %fusion.25, bf16[8,1152,256]{2,1,0:T(8,128)(2,1)} %bitcast.161, f32[8,1152,8,4,12]{1,4,3,2,0:T(8,128)} %get-tuple-element.57, f32[8,4,8,12]{3,1,0,2:T(4,128)S(1)} %get-tuple-element.56, pred[4,8,1152]{2,0,1:T(4,128)(4,1)S(1)} %compare_and_fusion, ...), kind=kOutput, calls=%fused_computation.23 | convolution fusion | flops 918552576 | bytes 24203264 | tf_op jit(solution)/shard_map/jtrhk,rkd->jtrhd/dot_general | solution.py:130
  109.3 0.9 copy.155
  110.6 24.9 %all_to_all.20 = bf16[16,4,8,1536]{3,2,1,0:T(8,128)(2,1)S(1)} all-to-all(bf16[16,4,8,1536]{3,2,1,0:T(8,128)(2,1)S(1)} %bitcast_select_fusion.1), channel_id=1, replica_groups=mesh['req'=8,'kv'=16] {'kv'}, dimensions={0} | all-to-all | bytes 3145728 | tf_op jit(solution)/shard_map/all_to_all | solution.py:160
  135.7 3.4 %multiply_reduce_fusion = (f32[32]{0:T(128)S(1)}, f32[32,1536]{1,0:T(8,128)S(1)}) fusion(bf16[1536,1536]{1,0:T(8,128)(2,1)} %param.23, bf16[4,8,1536]{2,1,0:T(8,128)(2,1)S(1)} %reduce_sum.322, f32[4,8,1536]{2,0,1:T(4,128)S(1)} %convert_bitcast_fusion), kind=kOutput, calls=%fused_computation.70 | convolution fusion | flops 151240672 | bytes 5210240 | tf_op jit(solution)/shard_map/dot_general | solution.py:165
  139.2 0.7 multiply_convert_fusion
  139.9 43.8 %all-gather.5.cloned.1.call-done = bf16[512,1536]{1,0:T(8,128)(2,1)} async-done(((bf16[32,1536]{1,0:T(8,128)(2,1)}), bf16[512,1536]{1,0:T(8,128)(2,1)}) %all-gather.5.cloned.1.call-update) | async-done | bytes 1572880 | tf_op jit(solution)/shard_map/all_gather | solution.py:169
  183.8 2.1 fusion.53
  185.8 4.2 %convolution_convert_fusion = bf16[512,1536]{1,0:T(8,128)(2,1)} fusion(bf16[288,1536]{1,0:T(8,128)(2,1)S(1)} %copy-done, bf16[512,1536]{1,0:T(8,128)(2,1)} %all-gather.5.cloned.1.call-done, bf16[1536,288]{0,1:T(8,128)(2,1)S(1)} %copy-done.3, f32[512,288]{0,1:T(8,128)S(1)} %fusion.53), kind=kOutput, calls=%fused_computation.12 | convolution fusion | flops 908230656 | bytes 5505024 | tf_op jit(solution)/shard_map/dot_general | solution.py:173
  190.1 4.7 %all-to-all-start.2 = ((bf16[16,32,1536]{2,1,0:T(8,128)(2,1)}), bf16[16,32,1536]{2,1,0:T(8,128)(2,1)S(1)}, u32[]{:S(2)}, u32[]{:S(2)}) async-start(bf16[16,32,1536]{2,1,0:T(8,128)(2,1)} %bitcast.168), calls=%async_computation.2 | async-start | bytes 3145728 | tf_op jit(solution)/shard_map/all_to_all | solution.py:175
  194.8 1.0 sort.32
  195.9 19.2 %all-to-all-done.2 = bf16[16,32,1536]{2,1,0:T(8,128)(2,1)S(1)} async-done(((bf16[16,32,1536]{2,1,0:T(8,128)(2,1)}), bf16[16,32,1536]{2,1,0:T(8,128)(2,1)S(1)}, u32[]{:S(2)}, u32[]{:S(2)}) %all-to-all-start.2) | async-done | bytes 1572896 | tf_op jit(solution)/shard_map/all_to_all | solution.py:175
  215.4 1.3 gather_fusion.4
  216.7 8.6 %all-to-all-start.3 = ((bf16[4,8,1,1536]{3,0,2,1:T(4,128)(2,1)}), bf16[4,8,1,1536]{3,0,2,1:T(4,128)(2,1)S(1)}, u32[]{:S(2)}, u32[]{:S(2)}) async-start(bf16[4,8,1,1536]{3,0,2,1:T(4,128)(2,1)} %bitcast.60), calls=%async_computation.3 | async-start | bytes 196608 | tf_op jit(solution)/shard_map/all_to_all | solution.py:182
  225.3 5.0 %all-to-all-done.3 = bf16[4,8,1,1536]{3,0,2,1:T(4,128)(2,1)S(1)} async-done(((bf16[4,8,1,1536]{3,0,2,1:T(4,128)(2,1)}), bf16[4,8,1,1536]{3,0,2,1:T(4,128)(2,1)S(1)}, u32[]{:S(2)}, u32[]{:S(2)}) %all-to-all-start.3) | async-done | bytes 98336 | tf_op jit(solution)/shard_map/all_to_all | solution.py:182
  (96 shorter events, 9.0 us)
Async XLA Ops:
  6.5 179.3 %copy-start = (bf16[288,1536]{1,0:T(8,128)(2,1)S(1)}, bf16[288,1536]{1,0:T(8,128)(2,1)}, u32[]{:S(2)}) copy-start(bf16[288,1536]{1,0:T(8,128)(2,1)} %param.27) | copy-start | bytes 2654212
  10.9 10.8 %all-to-all-start = ((bf16[4,8,1,1536]{3,0,2,1:T(4,128)(2,1)}), bf16[4,8,1,1536]{3,0,2,1:T(4,128)(2,1)S(1)}, u32[]{:S(2)}, u32[]{:S(2)}) async-start(bf16[4,8,1,1536]{3,0,2,1:T(4,128)(2,1)} %copy.127), calls=%async_computation | async-start | bytes 196608 | tf_op jit(solution)/shard_map/all_to_all | solution.py:80
  16.7 55.6 %all-gather.3.cloned.1.call-start = ((), (), s32[]{:S(2)}) async-start(), calls=%async_computation.4 | async-start | bytes 1949696 | tf_op jit(solution)/shard_map/all_gather | solution.py:88
  28.1 155.6 %all-gather.5.cloned.1.call-start = ((), (), s32[]{:S(2)}) async-start(), calls=%async_computation.5 | async-start | bytes 1671168 | tf_op jit(solution)/shard_map/all_gather | solution.py:169
  72.3 7.5 %slice-start = ((s8[4718592]{0:T(1024)(128)(4,1)}), s8[4194304]{0:T(1024)(128)(4,1)S(1)}, s32[]{:S(2)}) async-start(s8[4718592]{0:T(1024)(128)(4,1)} %bitcast.162), calls=%async_computation.6 | async-start | bytes 8388608
  76.2 3.6 %slice-start.1 = ((s8[4718592]{0:T(1024)(128)(4,1)}), s8[524288]{0:T(1024)(128)(4,1)S(1)}, s32[]{:S(2)}) async-start(s8[4718592]{0:T(1024)(128)(4,1)} %bitcast.162), calls=%async_computation.7 | async-start | bytes 1048576
  110.6 28.6 %copy-start.1 = (f32[1536]{0:T(1024)S(1)}, f32[1536]{0:T(1024)}, u32[]{:S(2)}) copy-start(f32[1536]{0:T(1024)} %param.24) | copy-start | bytes 18436
  135.7 48.1 %copy-start.2 = (bf16[1536,288]{0,1:T(8,128)(2,1)S(1)}, bf16[1536,288]{0,1:T(8,128)(2,1)}, u32[]{:S(2)}) copy-start(bf16[1536,288]{0,1:T(8,128)(2,1)} %param.25) | copy-start | bytes 2654212
  139.2 46.7 %copy-start.3 = (bf16[1536,288]{0,1:T(8,128)(2,1)S(1)}, bf16[1536,288]{0,1:T(8,128)(2,1)}, u32[]{:S(2)}) copy-start(bf16[1536,288]{0,1:T(8,128)(2,1)} %param.26) | copy-start | bytes 2654212
  190.1 25.0 %all-to-all-start.2 = ((bf16[16,32,1536]{2,1,0:T(8,128)(2,1)}), bf16[16,32,1536]{2,1,0:T(8,128)(2,1)S(1)}, u32[]{:S(2)}, u32[]{:S(2)}) async-start(bf16[16,32,1536]{2,1,0:T(8,128)(2,1)} %bitcast.168), calls=%async_computation.2 | async-start | bytes 3145728 | tf_op jit(solution)/shard_map/all_to_all | solution.py:175
  216.7 13.6 %all-to-all-start.3 = ((bf16[4,8,1,1536]{3,0,2,1:T(4,128)(2,1)}), bf16[4,8,1,1536]{3,0,2,1:T(4,128)(2,1)S(1)}, u32[]{:S(2)}, u32[]{:S(2)}) async-start(bf16[4,8,1,1536]{3,0,2,1:T(4,128)(2,1)} %bitcast.60), calls=%async_computation.3 | async-start | bytes 196608 | tf_op jit(solution)/shard_map/all_to_all | solution.py:182
Sparse Core Ops, SparseCore 0:
  28.3 44.0 all-gather.2
  140.1 43.6 all-gather.4
where the time goes:
time: 239 us; the launch traced here: 238 us
  waiting for transfers between devices  105 us (44%)
  matrix products  35.3 us (15%)
  blocking collectives  24.9 us (10%)
  local copies, waits for them, and re-layouts  20 us (8%)
  other arithmetic  20 us (8%)
  starting transfers between devices  19.1 us (8%)
  between operations  14 us (6%)
    all_gather x1, waiting for transfers between devices, on_device(): lax.all_gather(rms_round(residual, norm_mlp), 'kv', axis=0, tiled=True)  43.8 us
    all_gather x1, waiting for transfers between devices, on_device(): gathered = lax.all_gather(packed, 'kv', axis=0)  35.6 us
    all_to_all x1, blocking collectives, on_device(): lax.all_to_all(outgoing_att, 'kv', split_axis=0, concat_axis=0, tiled=True)  24.9 us
    all_to_all x1, waiting for transfers between devices, on_device(): lax.all_to_all(terms, 'kv', split_axis=0, concat_axis=0, tiled=True)  19.2 us
    reduce_sum x1, other arithmetic, on_device(): total_c = jnp.sum(weights.astype(jnp.float32), axis=-1)  11 us
    dot_general x1, matrix products, on_device(): jnp.einsum('jtrhk,rkd->jtrhd', weights, values, preferred_element_type=jn...  9.68 us
    all_to_all x1, starting transfers between devices, on_device(): lax.all_to_all(leaving, 'req', split_axis=1, concat_axis=1, tiled=True)  8.59 us
    dot_general x1, matrix products, on_device(): jnp.einsum('jtrhd,rkd->jtrhk', queries, keys, preferred_element_type=jnp....  8.53 us
  transfers between devices with their start and end apart: 5, of which 5 were waited for; matrix products, arithmetic and copies ran while one was open for 5% of the time, Pallas kernels for 0%

commit v1 on v0

--- a/solution.py
+++ b/solution.py
@@ -166,7 +166,11 @@
             attended_own.reshape(steps * rows, qwidth), w_out, preferred_element_type=jnp.float32
         )
     ).astype(jnp.bfloat16)
-    mlp_in = lax.all_gather(rms_round(residual, norm_mlp), "kv", axis=0, tiled=True)
+    content = rms_round(residual, norm_mlp)
+    p_next = jax.lax.all_to_all(
+        jnp.stack([content for _ in range(jax.lax.axis_size("kv"))]), "kv", 0, 0
+    )
+    mlp_in = jnp.concatenate(p_next, axis=0)
     gate = jnp.dot(mlp_in, w_gate, preferred_element_type=jnp.float32)
     upward = jnp.dot(mlp_in, w_up, preferred_element_type=jnp.float32)
     hidden = (jax.nn.gelu(gate, approximate=True) * upward).astype(jnp.bfloat16)

time: 239 us -> 213 us (0.89)
  waiting for transfers between devices: 105 us -> 59.4 us
  blocking collectives: 24.9 us -> 46.8 us
    all_gather x1 -> x0, waiting for transfers between devices: 43.8 us -> none  [on_device(): lax.all_gather(rms_round(residual, norm_mlp), 'kv', axis=0, tiled=True)]
    all_to_all x0 -> x1, blocking collectives: none -> 21.9 us  [on_device(): jax.lax.all_to_all(jnp.stack([content for _ in range(jax.lax.axis_size('k...]
  transfers between devices with their start and end apart: 5 -> 4, of which waited for: 5 -> 4; matrix products, arithmetic and copies ran while one was open for 5% -> 6% of each run, Pallas kernels for 0% -> 0%
where the time goes in v1:
time: 213 us
  waiting for transfers between devices  59.4 us (28%)
  blocking collectives  46.8 us (22%)
  matrix products  33.6 us (16%)
  local copies, waits for them, and re-layouts  20.2 us (9%)
  other arithmetic  19.4 us (9%)
  starting transfers between devices  19.3 us (9%)
  between operations  13.9 us (7%)
    all_gather x1, waiting for transfers between devices, on_device(): gathered = lax.all_gather(packed, 'kv', axis=0)  35.7 us
    all_to_all x1, blocking collectives, on_device(): lax.all_to_all(outgoing_att, 'kv', split_axis=0, concat_axis=0, tiled=True)  24.9 us
    all_to_all x1, blocking collectives, on_device(): jax.lax.all_to_all(jnp.stack([content for _ in range(jax.lax.axis_size('k...  21.9 us
    all_to_all x1, waiting for transfers between devices, on_device(): lax.all_to_all(terms, 'kv', split_axis=0, concat_axis=0, tiled=True)  17.1 us
    reduce_sum x1, other arithmetic, on_device(): total_c = jnp.sum(weights.astype(jnp.float32), axis=-1)  11 us
    all_to_all x1, starting transfers between devices, on_device(): lax.all_to_all(leaving, 'req', split_axis=1, concat_axis=1, tiled=True)  9.79 us
    dot_general x1, matrix products, on_device(): jnp.einsum('jtrhk,rkd->jtrhd', weights, values, preferred_element_type=jn...  9.68 us
    dot_general x1, matrix products, on_device(): jnp.einsum('jtrhd,rkd->jtrhk', queries, keys, preferred_element_type=jnp....  8.53 us
  transfers between devices with their start and end apart: 4, of which 4 were waited for; matrix products, arithmetic and copies ran while one was open for 6% of the time, Pallas kernels for 0%

profile of v1, /device:TPU:1, one launch (start us, length us, event | category | flops | bytes accessed | tf_op | source)
XLA Modules:
  0.0 212.6 jit_solution(10077016287649858722)
XLA Ops:
  6.5 0.8 reshape.457
  7.5 1.0 sort.31
  8.5 1.7 gather_fusion
  10.3 0.7 copy.127
  10.9 5.8 %all-to-all-start = ((bf16[4,8,1,1536]{3,0,2,1:T(4,128)(2,1)}), bf16[4,8,1,1536]{3,0,2,1:T(4,128)(2,1)S(1)}, u32[]{:S(2)}, u32[]{:S(2)}) async-start(bf16[4,8,1,1536]{3,0,2,1:T(4,128)(2,1)} %copy.127), calls=%async_computation | async-start | bytes 196608 | tf_op jit(solution)/shard_map/all_to_all | solution.py:80
  16.9 0.7 compare_select_fusion
  17.9 0.7 constant_dynamic-slice_fusion.4
  18.8 1.3 gather_fusion.3
  20.2 1.6 all-to-all-done
  22.7 1.4 convolution_convert_fusion.2
  24.1 3.3 %convolution_convert_fusion.1 = bf16[32,1536]{1,0:T(8,128)(2,1)S(1)} fusion(bf16[1536,1536]{1,0:T(8,128)(2,1)} %param.21, f32[4,8,1536]{2,0,1:T(4,128)S(1)} %convert_bitcast_fusion, f32[1536]{0:T(1024)} %param.20, f32[32]{0:T(128)S(1)} %rsqrt.20), kind=kOutput, calls=%fused_computation.19 | convolution fusion | flops 151191552 | bytes 5019776 | tf_op jit(solution)/shard_map/dot_general | solution.py:85
  28.1 7.8 %gather_fusion.2 = bf16[72,128,256]{2,1,0:T(8,128)(2,1)} fusion(bf16[72,128,256]{2,1,0:T(8,128)(2,1)} %param.19, s32[1024]{0:T(1024)S(1)} %pad_clamp_fusion.3), kind=kCustom, calls=%fused_computation.2 | custom fusion | bytes 9437472 | tf_op jit(solution)/shard_map/gather | solution.py:115
  36.7 35.7 %all-gather.2.cloned.1.call-done = bf16[16,4,8,1792]{3,2,1,0:T(8,128)(2,1)} async-done(((bf16[1,4,8,1792]{3,2,1,0:T(8,128)(2,1)}), bf16[16,4,8,1792]{3,2,1,0:T(8,128)(2,1)}) %all-gather.2.cloned.1.call-update) | async-done | bytes 1835024 | tf_op jit(solution)/shard_map/all_gather | solution.py:88
  72.3 1.4 constant_dynamic-slice_fusion.1
  73.8 0.8 select_reduce_fusion.9
  76.6 0.7 fusion.52
  77.9 1.9 fusion.25
  79.8 8.5 %fusion = (f32[8,4,8,12]{3,1,0,2:T(4,128)S(1)}, f32[8,1152,8,4,12]{1,4,3,2,0:T(8,128)}) fusion(pred[4,8,1152]{2,0,1:T(4,128)(4,1)S(1)} %compare_and_fusion, bf16[8,4,8,12,128]{4,2,3,1,0:T(8,128)(2,1)S(1)} %slice_bitcast_fusion.6, bf16[8,1152,256]{2,1,0:T(8,128)(2,1)S(1)} %bitcast.165), kind=kOutput, calls=%fused_computation.10 | convolution fusion | flops 916583424 | bytes 17350656 | tf_op jit(solution)/shard_map/jtrhd,rkd->jtrhk/dot_general | solution.py:120
  88.3 11.0 %convert_reduce_fusion = f32[8,4,8,12]{3,1,0,2:T(4,128)S(1)} fusion(f32[8,4,8,12]{3,1,0,2:T(4,128)S(1)} %get-tuple-element.56, f32[8,1152,8,4,12]{1,4,3,2,0:T(8,128)} %get-tuple-element.57, pred[4,8,1152]{2,0,1:T(4,128)(4,1)S(1)} %compare_and_fusion), kind=kLoop, calls=%fused_computation.8 | loop fusion | flops 17691648 | bytes 14217216 | tf_op jit(solution)/shard_map/reduce_sum | solution.py:129
  99.7 9.7 %fusion.6 = bf16[8,4,8,12,128]{4,3,1,0,2:T(8,128)(2,1)S(1)} fusion(f32[8,4,8,12,128]{4,3,1,0,2:T(8,128)} %fusion.25, bf16[8,1152,256]{2,1,0:T(8,128)(2,1)} %bitcast.162, f32[8,1152,8,4,12]{1,4,3,2,0:T(8,128)} %get-tuple-element.57, f32[8,4,8,12]{3,1,0,2:T(4,128)S(1)} %get-tuple-element.56, pred[4,8,1152]{2,0,1:T(4,128)(4,1)S(1)} %compare_and_fusion, ...), kind=kOutput, calls=%fused_computation.23 | convolution fusion | flops 918552576 | bytes 24203264 | tf_op jit(solution)/shard_map/jtrhk,rkd->jtrhd/dot_general | solution.py:130
  109.3 0.9 copy.155
  110.6 24.9 %all_to_all.25 = bf16[16,4,8,1536]{3,2,1,0:T(8,128)(2,1)S(1)} all-to-all(bf16[16,4,8,1536]{3,2,1,0:T(8,128)(2,1)S(1)} %bitcast_select_fusion.1), channel_id=1, replica_groups=mesh['req'=8,'kv'=16] {'kv'}, dimensions={0} | all-to-all | bytes 3145728 | tf_op jit(solution)/shard_map/all_to_all | solution.py:160
  135.8 3.4 %multiply_reduce_fusion = (f32[32]{0:T(128)S(1)}, f32[32,1536]{1,0:T(8,128)S(1)}) fusion(bf16[1536,1536]{1,0:T(8,128)(2,1)} %param.23, bf16[4,8,1536]{2,1,0:T(8,128)(2,1)S(1)} %reduce_sum.322, f32[4,8,1536]{2,0,1:T(4,128)S(1)} %convert_bitcast_fusion), kind=kOutput, calls=%fused_computation.70 | convolution fusion | flops 151240672 | bytes 5210240 | tf_op jit(solution)/shard_map/dot_general | solution.py:165
  139.5 21.9 %all_to_all.26 = bf16[16,32,1536]{2,1,0:T(8,128)(2,1)S(1)} all-to-all(bf16[16,32,1536]{2,1,0:T(8,128)(2,1)S(1)} %stack.115), channel_id=1, replica_groups=mesh['req'=8,'kv'=16] {'kv'}, dimensions={0} | all-to-all | bytes 3145728 | tf_op jit(solution)/shard_map/all_to_all | solution.py:170
  162.1 4.0 %convolution_convert_fusion = bf16[512,1536]{1,0:T(8,128)(2,1)} fusion(bf16[288,1536]{1,0:T(8,128)(2,1)S(1)} %copy-done, bf16[512,1536]{1,0:T(8,128)(2,1)S(1)} %bitcast.171, bf16[1536,288]{0,1:T(8,128)(2,1)} %param.26, f32[512,288]{0,1:T(8,128)S(1)} %fusion.53), kind=kOutput, calls=%fused_computation.12 | convolution fusion | flops 908230656 | bytes 5505024 | tf_op jit(solution)/shard_map/dot_general | solution.py:177
  166.1 3.7 %all-to-all-start.3 = ((bf16[16,32,1536]{2,1,0:T(8,128)(2,1)}), bf16[16,32,1536]{2,1,0:T(8,128)(2,1)S(1)}, u32[]{:S(2)}, u32[]{:S(2)}) async-start(bf16[16,32,1536]{2,1,0:T(8,128)(2,1)} %bitcast.169), calls=%async_computation.3 | async-start | bytes 3145728 | tf_op jit(solution)/shard_map/all_to_all | solution.py:179
  169.8 1.0 sort.32
  171.0 17.1 %all-to-all-done.3 = bf16[16,32,1536]{2,1,0:T(8,128)(2,1)S(1)} async-done(((bf16[16,32,1536]{2,1,0:T(8,128)(2,1)}), bf16[16,32,1536]{2,1,0:T(8,128)(2,1)S(1)}, u32[]{:S(2)}, u32[]{:S(2)}) %all-to-all-start.3) | async-done | bytes 1572896 | tf_op jit(solution)/shard_map/all_to_all | solution.py:179
  188.4 1.3 gather_fusion.4
  189.7 9.8 %all-to-all-start.4 = ((bf16[4,8,1,1536]{3,0,2,1:T(4,128)(2,1)}), bf16[4,8,1,1536]{3,0,2,1:T(4,128)(2,1)S(1)}, u32[]{:S(2)}, u32[]{:S(2)}) async-start(bf16[4,8,1,1536]{3,0,2,1:T(4,128)(2,1)} %bitcast.61), calls=%async_computation.4 | async-start | bytes 196608 | tf_op jit(solution)/shard_map/all_to_all | solution.py:186
  199.5 5.0 %all-to-all-done.4 = bf16[4,8,1,1536]{3,0,2,1:T(4,128)(2,1)S(1)} async-done(((bf16[4,8,1,1536]{3,0,2,1:T(4,128)(2,1)}), bf16[4,8,1,1536]{3,0,2,1:T(4,128)(2,1)S(1)}, u32[]{:S(2)}, u32[]{:S(2)}) %all-to-all-start.4) | async-done | bytes 98336 | tf_op jit(solution)/shard_map/all_to_all | solution.py:186
  205.1 0.7 copy.158
  (93 shorter events, 8.5 us)
Async XLA Ops:
  6.5 155.5 %copy-start = (bf16[288,1536]{1,0:T(8,128)(2,1)S(1)}, bf16[288,1536]{1,0:T(8,128)(2,1)}, u32[]{:S(2)}) copy-start(bf16[288,1536]{1,0:T(8,128)(2,1)} %param.27) | copy-start | bytes 2654212
  10.9 10.8 %all-to-all-start = ((bf16[4,8,1,1536]{3,0,2,1:T(4,128)(2,1)}), bf16[4,8,1,1536]{3,0,2,1:T(4,128)(2,1)S(1)}, u32[]{:S(2)}, u32[]{:S(2)}) async-start(bf16[4,8,1,1536]{3,0,2,1:T(4,128)(2,1)} %copy.127), calls=%async_computation | async-start | bytes 196608 | tf_op jit(solution)/shard_map/all_to_all | solution.py:80
  16.7 55.6 %all-gather.2.cloned.1.call-start = ((), (), s32[]{:S(2)}) async-start(), calls=%async_computation.5 | async-start | bytes 1949696 | tf_op jit(solution)/shard_map/all_gather | solution.py:88
  72.3 7.5 %slice-start = ((s8[4718592]{0:T(1024)(128)(4,1)}), s8[4194304]{0:T(1024)(128)(4,1)S(1)}, s32[]{:S(2)}) async-start(s8[4718592]{0:T(1024)(128)(4,1)} %bitcast.163), calls=%async_computation.6 | async-start | bytes 8388608
  76.2 3.6 %slice-start.1 = ((s8[4718592]{0:T(1024)(128)(4,1)}), s8[524288]{0:T(1024)(128)(4,1)S(1)}, s32[]{:S(2)}) async-start(s8[4718592]{0:T(1024)(128)(4,1)} %bitcast.163), calls=%async_computation.7 | async-start | bytes 1048576
  110.6 28.6 %copy-start.1 = (f32[1536]{0:T(1024)S(1)}, f32[1536]{0:T(1024)}, u32[]{:S(2)}) copy-start(f32[1536]{0:T(1024)} %param.24) | copy-start | bytes 18436
  135.7 25.7 %copy-start.2 = (bf16[1536,288]{0,1:T(8,128)(2,1)S(1)}, bf16[1536,288]{0,1:T(8,128)(2,1)}, u32[]{:S(2)}) copy-start(bf16[1536,288]{0,1:T(8,128)(2,1)} %param.25) | copy-start | bytes 2654212
  166.1 22.0 %all-to-all-start.3 = ((bf16[16,32,1536]{2,1,0:T(8,128)(2,1)}), bf16[16,32,1536]{2,1,0:T(8,128)(2,1)S(1)}, u32[]{:S(2)}, u32[]{:S(2)}) async-start(bf16[16,32,1536]{2,1,0:T(8,128)(2,1)} %bitcast.169), calls=%async_computation.3 | async-start | bytes 3145728 | tf_op jit(solution)/shard_map/all_to_all | solution.py:179
  189.7 14.8 %all-to-all-start.4 = ((bf16[4,8,1,1536]{3,0,2,1:T(4,128)(2,1)}), bf16[4,8,1,1536]{3,0,2,1:T(4,128)(2,1)S(1)}, u32[]{:S(2)}, u32[]{:S(2)}) async-start(bf16[4,8,1,1536]{3,0,2,1:T(4,128)(2,1)} %bitcast.61), calls=%async_computation.4 | async-start | bytes 196608 | tf_op jit(solution)/shard_map/all_to_all | solution.py:186
Sparse Core Ops, SparseCore 0:
  28.3 44.0 all-gather.1
